TPU v7x, 32 devices: a whole 2x2x4 slice. The times are simulated.
32 devices in a mesh: row: 4 (over y, x), col: 8 (over z, core).
Axes of the slice: x: 2, y: 2, z: 4, core: 2. Of those that a mesh axis runs over, the one named last changes fastest.
Arguments:
- matrix_in: bfloat16 [2048, 2048], P('row', 'col'), as said below
- pattern: int32 [16, 16], replicated, may hold values from 0 to 1, as said below
Outputs:
- sign_step: float32 [2048, 2048], P('row', 'col')
Inputs may be any that keep to these rules, and one draw needn't show every extreme that they name: `pattern`: symmetric, every diagonal block is 1, and every block (i, (i + 8) mod 16) is 1. `matrix_in`: exactly symmetric.
All inputs are finite; a program needn't handle non-finite values.
Results may differ from a plain program's by a relative error of at most 0.0029.
Values may be sent and summed in bfloat16 or wider, within the bound.
No kernel may reach another device: no remote copies, remote signals or barrier semaphores. Data moves between devices by JAX's collectives and lax.ppermute only.
A program may use at most 64 MiB of HBM per device.

v0:
```python
import jax
import jax.numpy as jnp
from jax import lax
from jax.sharding import PartitionSpec as P

B = 128


def body(matrix_in, pattern):
    block_rows = matrix_in.shape[0] // B
    block_cols = matrix_in.shape[1] // B
    row_index = lax.axis_index("row")
    col_index = lax.axis_index("col")
    local_blocks = lax.dynamic_slice(
        pattern, (row_index * block_rows, col_index * block_cols), (block_rows, block_cols)
    )
    local_mask = jnp.repeat(jnp.repeat(local_blocks, B, axis=0), B, axis=1)
    masked = matrix_in * local_mask.astype(jnp.bfloat16)
    rows_all = lax.all_gather(masked, "col", axis=1, tiled=True)
    left_part = rows_all
    square = jnp.dot(
        left_part,
        lax.all_gather(masked, "row", axis=0, tiled=True),
        preferred_element_type=jnp.float32,
    )
    mask_float = local_mask.astype(jnp.float32)
    filtered = (mask_float * square).astype(jnp.bfloat16)
    left_part = rows_all
    cubic = jnp.dot(
        left_part,
        lax.all_gather(filtered, "row", axis=0, tiled=True),
        preferred_element_type=jnp.float32,
    )
    return mask_float * (1.5 * masked.astype(jnp.float32) - 0.5 * cubic)


def solution(mesh):
    return jax.shard_map(
        body, mesh=mesh, in_specs=(P("row", "col"), P()), out_specs=P("row", "col"), check_vma=False
    )
```

profile of v0, /device:TPU:0, one launch (start us, length us, event | category | flops | bytes accessed | tf_op | source)
XLA Modules:
  0.0 110.8 jit_solution(12114034085471506654)
XLA Ops:
  6.5 0.0 all-gather.6.cloned.1.call-start
  6.5 0.8 dynamic-slice_convert_fusion.1
  7.3 0.6 broadcast_in_dim.13
  7.9 1.7 %bitcast_multiply_fusion = bf16[512,256]{1,0:T(8,128)(2,1)} fusion(bf16[512,256]{1,0:T(8,128)(2,1)} %param.2, bf16[64,8,2,128]{3,2,1,0:T(2,128)(2,1)S(1)} %bitcast.13), kind=kLoop, calls=%fused_computation.5 | loop fusion | flops 131072 | bytes 786432 | tf_op jit(solution)/shard_map/mul | solution.py:18
  9.6 0.0 all-gather.6.cloned.1.call-update
  9.6 0.0 all-gather.4.cloned.1.call-start
  9.7 0.7 all-gather.4.cloned.1.call-update
  10.4 0.0 all-gather.8.cloned.1.call-start
  10.4 28.7 %all-gather.6.cloned.1.call-done = bf16[2048,256]{1,0:T(8,128)(2,1)} async-done(((bf16[512,256]{1,0:T(8,128)(2,1)}), bf16[2048,256]{1,0:T(8,128)(2,1)}) %all-gather.6.cloned.1.call-update) | async-done | bytes 1048592 | tf_op jit(solution)/shard_map/all_gather | solution.py:23
  39.1 32.5 %all-gather.4.cloned.1.call-done = bf16[512,2048]{1,0:T(8,128)(2,1)} async-done(((bf16[512,256]{1,0:T(8,128)(2,1)}), bf16[512,2048]{1,0:T(8,128)(2,1)}) %all-gather.4.cloned.1.call-update) | async-done | bytes 2097168 | tf_op jit(solution)/shard_map/all_gather | solution.py:19
  71.6 0.6 broadcast_in_dim.11
  72.2 0.0 copy-start
  72.2 0.0 copy-start.1
  72.2 3.4 %fusion.2 = bf16[512,256]{1,0:T(8,128)(2,1)} fusion(bf16[512,2048]{1,0:T(8,128)(2,1)} %all-gather.4.cloned.1.call-done, bf16[2048,256]{1,0:T(8,128)(2,1)} %all-gather.6.cloned.1.call-done, f32[64,8,2,128]{3,2,1,0:T(2,128)S(1)} %bitcast.16), kind=kOutput, calls=%fused_computation.4 | convolution fusion | flops 537133056 | bytes 3932160 | tf_op jit(solution)/shard_map/dot_general | solution.py:21
  75.7 0.0 all-gather.8.cloned.1.call-update
  75.7 25.9 %all-gather.8.cloned.1.call-done = bf16[2048,256]{1,0:T(8,128)(2,1)} async-done(((bf16[512,256]{1,0:T(8,128)(2,1)}), bf16[2048,256]{1,0:T(8,128)(2,1)}) %all-gather.8.cloned.1.call-update) | async-done | bytes 1048592 | tf_op jit(solution)/shard_map/all_gather | solution.py:31
  101.5 0.0 copy-done
  101.5 0.0 copy-done.1
  101.5 2.7 %fusion.1 = f32[512,256]{1,0:T(8,128)} fusion(bf16[512,2048]{1,0:T(8,128)(2,1)S(1)} %copy-done.1, bf16[2048,256]{1,0:T(8,128)(2,1)} %all-gather.8.cloned.1.call-done, bf16[512,256]{1,0:T(8,128)(2,1)S(1)} %copy-done, f32[64,8,2,128]{3,2,1,0:T(2,128)S(1)} %bitcast.17), kind=kOutput, calls=%fused_computation.3 | convolution fusion | flops 537526272 | bytes 4456448 | tf_op jit(solution)/shard_map/dot_general | solution.py:29
  (2 shorter events, 0.0 us)
Async XLA Ops:
  6.5 32.6 %all-gather.6.cloned.1.call-start = ((), (), s32[]{:S(2)}) async-start(), calls=%async_computation.1 | async-start | bytes 1310720 | tf_op jit(solution)/shard_map/all_gather | solution.py:23
  9.6 61.9 %all-gather.4.cloned.1.call-start = ((), (), s32[]{:S(2)}) async-start(), calls=%async_computation | async-start | bytes 2359296 | tf_op jit(solution)/shard_map/all_gather | solution.py:19
  10.4 91.1 %all-gather.8.cloned.1.call-start = ((), (), s32[]{:S(2)}) async-start(), calls=%async_computation.2 | async-start | bytes 1310720 | tf_op jit(solution)/shard_map/all_gather | solution.py:31
  72.2 29.3 %copy-start = (bf16[512,256]{1,0:T(8,128)(2,1)S(1)}, bf16[512,256]{1,0:T(8,128)(2,1)}, u32[]{:S(2)}) copy-start(bf16[512,256]{1,0:T(8,128)(2,1)} %bitcast_multiply_fusion) | copy-start | bytes 786436
  72.2 29.3 %copy-start.1 = (bf16[512,2048]{1,0:T(8,128)(2,1)S(1)}, bf16[512,2048]{1,0:T(8,128)(2,1)}, u32[]{:S(2)}) copy-start(bf16[512,2048]{1,0:T(8,128)(2,1)} %all-gather.4.cloned.1.call-done) | copy-start | bytes 6291460
Sparse Core Ops, SparseCore 0:
  9.8 29.3 all-gather.5
  40.7 30.8 all-gather.3
  75.8 25.6 all-gather.7
where the time goes:
time: 111 us
  waiting for transfers between devices  87.7 us (79%)
  between operations  13.1 us (12%)
  matrix products  6.16 us (6%)
  other arithmetic  2.45 us (2%)
  local copies, waits for them, and re-layouts  1.25 us (1%)
    all_gather x1, waiting for transfers between devices, body(): rows_all = lax.all_gather(masked, 'col', axis=1, tiled=True)  32.5 us
    all_gather x1, waiting for transfers between devices, body(): lax.all_gather(masked, 'row', axis=0, tiled=True)  28.7 us
    all_gather x1, waiting for transfers between devices, body(): lax.all_gather(filtered, 'row', axis=0, tiled=True)  25.9 us
    dot_general x1, matrix products, body(): jnp.dot(left_part, lax.all_gather(masked, 'row', axis=0, tiled=True), pre...  3.43 us
    dot_general x1, matrix products, body(): jnp.dot(left_part, lax.all_gather(filtered, 'row', axis=0, tiled=True), p...  2.73 us
  transfers between devices with their start and end apart: 3, of which 3 were waited for; matrix products, arithmetic and copies ran while one was open for 0% of the time, Pallas kernels for 0%

commit v1 on v0

--- a/solution.py
+++ b/solution.py
@@ -4,6 +4,21 @@
 from jax.sharding import PartitionSpec as P
 
 B = 128
+
+
+def mark_slabs(chip_axis, join_dim, mine):
+    width = lax.axis_size(chip_axis)
+    fields = [mine]
+    to_i = 1
+    while to_i < width:
+        d_next = lax.ppermute(
+            fields[to_i - 1], chip_axis, [(at, (at - 1) % width) for at in range(width)]
+        )
+        fields.append(d_next)
+        to_i += 1
+    far_arr = jnp.concatenate(fields, join_dim)
+    s_next = lax.axis_index(chip_axis)
+    return jnp.roll(far_arr, s_next * mine.shape[join_dim], join_dim)
 
 
 def body(matrix_in, pattern):
@@ -18,11 +33,7 @@
     masked = matrix_in * local_mask.astype(jnp.bfloat16)
     rows_all = lax.all_gather(masked, "col", axis=1, tiled=True)
     left_part = rows_all
-    square = jnp.dot(
-        left_part,
-        lax.all_gather(masked, "row", axis=0, tiled=True),
-        preferred_element_type=jnp.float32,
-    )
+    square = jnp.dot(left_part, mark_slabs("row", 0, masked), preferred_element_type=jnp.float32)
     mask_float = local_mask.astype(jnp.float32)
     filtered = (mask_float * square).astype(jnp.bfloat16)
     left_part = rows_all

time: 111 us -> 83.4 us (0.75)
  waiting for transfers between devices: 87.7 us -> 47.8 us
  starting transfers between devices: 0.08 us -> 10.6 us
    all_gather x1 -> x0, waiting for transfers between devices: 28.7 us -> none  [body(): lax.all_gather(masked, 'row', axis=0, tiled=True)]
    all_gather x1, waiting for transfers between devices: 32.5 us -> 7.5 us  [body(): rows_all = lax.all_gather(masked, 'col', axis=1, tiled=True)]
    ppermute x0 -> x3, waiting for transfers between devices: none -> 14.4 us  [mark_slabs(): lax.ppermute(fields[to_i - 1], chip_axis, [(at, (at - 1) % width) for at...]
    ppermute x0 -> x3, starting transfers between devices: none -> 10.6 us  [mark_slabs(): lax.ppermute(fields[to_i - 1], chip_axis, [(at, (at - 1) % width) for at...]
    unnamed x0 -> x1, other arithmetic: none -> 1.73 us
    mul x1 -> x0, other arithmetic: 1.69 us -> none  [body(): masked = matrix_in * local_mask.astype(jnp.bfloat16)]
  transfers between devices with their start and end apart: 3 -> 5, of which waited for: 3 -> 5; matrix products, arithmetic and copies ran while one was open for 0% -> 1% of each run, Pallas kernels for 0% -> 0%
where the time goes in v1:
time: 83.4 us; the launch traced here: 83.2 us
  waiting for transfers between devices  47.8 us (57%)
  between operations  13.5 us (16%)
  starting transfers between devices  10.6 us (13%)
  matrix products  6.43 us (8%)
  other arithmetic  2.49 us (3%)
  local copies, waits for them, and re-layouts  2.33 us (3%)
    all_gather x1, waiting for transfers between devices, body(): lax.all_gather(filtered, 'row', axis=0, tiled=True)  25.9 us
    ppermute x3, waiting for transfers between devices, mark_slabs(): lax.ppermute(fields[to_i - 1], chip_axis, [(at, (at - 1) % width) for at...  14.4 us
    ppermute x3, starting transfers between devices, mark_slabs(): lax.ppermute(fields[to_i - 1], chip_axis, [(at, (at - 1) % width) for at...  10.6 us
    all_gather x1, waiting for transfers between devices, body(): rows_all = lax.all_gather(masked, 'col', axis=1, tiled=True)  7.5 us
    dot_general x1, matrix products, body(): jnp.dot(left_part, lax.all_gather(filtered, 'row', axis=0, tiled=True), p...  3.36 us
    dot_general x1, matrix products, body(): jnp.dot(left_part, mark_slabs('row', 0, masked), preferred_element_type=j...  3.07 us
    unnamed x1, other arithmetic  1.73 us
  transfers between devices with their start and end apart: 5, of which 5 were waited for; matrix products, arithmetic and copies ran while one was open for 1% of the time, Pallas kernels for 0%

profile of v1, /device:TPU:0, one launch (start us, length us, event | category | flops | bytes accessed | tf_op | source)
XLA Modules:
  0.0 83.2 jit_solution(133203701422132999)
XLA Ops:
  6.5 0.0 all-gather.3.cloned.1.call-start
  6.5 0.8 dynamic-slice_convert_fusion.1
  7.3 0.6 broadcast_in_dim.13
  7.9 1.7 %constant_dynamic-update-slice_fusion.7 = (bf16[4096,256]{1,0:T(8,128)(2,1)S(1)}, bf16[512,256]{1,0:T(8,128)(2,1)}) fusion(bf16[512,256]{1,0:T(8,128)(2,1)} %param.2, bf16[64,8,2,128]{3,2,1,0:T(2,128)(2,1)S(1)} %bitcast.14), kind=kLoop, calls=%fused_computation.14 | loop fusion | flops 524287 | bytes 1048576
  9.7 0.0 all-gather.3.cloned.1.call-update
  9.7 0.0 all-gather.5.cloned.1.call-start
  9.7 3.9 %collective-permute-start = (bf16[512,256]{1,0:T(8,128)(2,1)}, bf16[512,256]{1,0:T(8,128)(2,1)S(1)}, u32[]{:S(2)}, u32[]{:S(2)}) collective-permute-start(bf16[512,256]{1,0:T(8,128)(2,1)} %get-tuple-element.6), channel_id=1, source_target_pairs={{0,24},{8,0},{16,8},{24,16},{1,25},{9,1},{17,9},{25,17},{2,26},{10... | collective-permute-start | bytes 786440 | tf_op jit(solution)/shard_map/ppermute | solution.py:14
  13.7 5.9 %collective-permute-done = bf16[512,256]{1,0:T(8,128)(2,1)S(1)} collective-permute-done((bf16[512,256]{1,0:T(8,128)(2,1)}, bf16[512,256]{1,0:T(8,128)(2,1)S(1)}, u32[]{:S(2)}, u32[]{:S(2)}) %collective-permute-start) | collective-permute-done | bytes 262176 | tf_op jit(solution)/shard_map/ppermute | solution.py:14
  19.6 3.3 %collective-permute-start.1 = (bf16[512,256]{1,0:T(8,128)(2,1)S(1)}, bf16[512,256]{1,0:T(8,128)(2,1)S(1)}, u32[]{:S(2)}, u32[]{:S(2)}) collective-permute-start(bf16[512,256]{1,0:T(8,128)(2,1)S(1)} %collective-permute-done), channel_id=1, source_target_pairs={{0,24},{8,0},{16,8},{24,16},{1,25},{9,1},{17,9},{25,17},{2,26},{10... | collective-permute-start | bytes 786440 | tf_op jit(solution)/shard_map/ppermute | solution.py:14
  22.8 4.7 %collective-permute-done.1 = bf16[512,256]{1,0:T(8,128)(2,1)S(1)} collective-permute-done((bf16[512,256]{1,0:T(8,128)(2,1)S(1)}, bf16[512,256]{1,0:T(8,128)(2,1)S(1)}, u32[]{:S(2)}, u32[]{:S(2)}) %collective-permute-start.1) | collective-permute-done | bytes 262176 | tf_op jit(solution)/shard_map/ppermute | solution.py:14
  27.5 3.4 %collective-permute-start.2 = (bf16[512,256]{1,0:T(8,128)(2,1)S(1)}, bf16[512,256]{1,0:T(8,128)(2,1)S(1)}, u32[]{:S(2)}, u32[]{:S(2)}) collective-permute-start(bf16[512,256]{1,0:T(8,128)(2,1)S(1)} %collective-permute-done.1), channel_id=1, source_target_pairs={{0,24},{8,0},{16,8},{24,16},{1,25},{9,1},{17,9},{25,17},{2,26},{10... | collective-permute-start | bytes 786440 | tf_op jit(solution)/shard_map/ppermute | solution.py:14
  31.0 3.8 %collective-permute-done.2 = bf16[512,256]{1,0:T(8,128)(2,1)S(1)} collective-permute-done((bf16[512,256]{1,0:T(8,128)(2,1)S(1)}, bf16[512,256]{1,0:T(8,128)(2,1)S(1)}, u32[]{:S(2)}, u32[]{:S(2)}) %collective-permute-start.2) | collective-permute-done | bytes 262176 | tf_op jit(solution)/shard_map/ppermute | solution.py:14
  34.8 1.0 %constant_dynamic-update-slice_fusion.3 = bf16[4096,256]{1,0:T(8,128)(2,1)S(1)} fusion(bf16[4096,256]{1,0:T(8,128)(2,1)S(1)} %constant_dynamic-update-slice_fusion.4, bf16[512,256]{1,0:T(8,128)(2,1)} %get-tuple-element.6), kind=kLoop, calls=%fused_computation.10 | loop fusion | bytes 524288
  35.9 7.5 %all-gather.3.cloned.1.call-done = bf16[512,2048]{1,0:T(8,128)(2,1)} async-done(((bf16[512,256]{1,0:T(8,128)(2,1)}), bf16[512,2048]{1,0:T(8,128)(2,1)}) %all-gather.3.cloned.1.call-update) | async-done | bytes 2097168 | tf_op jit(solution)/shard_map/all_gather | solution.py:34
  43.4 0.6 broadcast_in_dim.11
  44.0 0.0 copy-start
  44.0 3.1 %fusion.2 = bf16[512,256]{1,0:T(8,128)(2,1)} fusion(bf16[512,2048]{1,0:T(8,128)(2,1)} %all-gather.3.cloned.1.call-done, bf16[4096,256]{1,0:T(8,128)(2,1)S(1)} %constant_dynamic-update-slice_fusion, s32[]{:T(128)S(6)} %select_n.22, f32[64,8,2,128]{3,2,1,0:T(2,128)S(1)} %bitcast.16), kind=kOutput, calls=%fused_computation.4 | convolution fusion | flops 537133056 | bytes 3932164 | tf_op jit(solution)/shard_map/dot_general | solution.py:36
  47.1 0.0 all-gather.5.cloned.1.call-update
  47.1 25.9 %all-gather.5.cloned.1.call-done = bf16[2048,256]{1,0:T(8,128)(2,1)} async-done(((bf16[512,256]{1,0:T(8,128)(2,1)}), bf16[2048,256]{1,0:T(8,128)(2,1)}) %all-gather.5.cloned.1.call-update) | async-done | bytes 1048592 | tf_op jit(solution)/shard_map/all_gather | solution.py:42
  73.0 0.0 copy-done
  73.0 3.4 %fusion.1 = f32[512,256]{1,0:T(8,128)} fusion(bf16[512,2048]{1,0:T(8,128)(2,1)} %all-gather.3.cloned.1.call-done, bf16[2048,256]{1,0:T(8,128)(2,1)} %all-gather.5.cloned.1.call-done, bf16[512,256]{1,0:T(8,128)(2,1)S(1)} %copy-done, f32[64,8,2,128]{3,2,1,0:T(2,128)S(1)} %bitcast.17), kind=kOutput, calls=%fused_computation.3 | convolution fusion | flops 537526272 | bytes 4456448 | tf_op jit(solution)/shard_map/dot_general | solution.py:40
  (8 shorter events, 0.2 us)
Async XLA Ops:
  6.5 36.8 %all-gather.3.cloned.1.call-start = ((), (), s32[]{:S(2)}) async-start(), calls=%async_computation | async-start | bytes 2359296 | tf_op jit(solution)/shard_map/all_gather | solution.py:34
  9.7 63.3 %all-gather.5.cloned.1.call-start = ((), (), s32[]{:S(2)}) async-start(), calls=%async_computation.1 | async-start | bytes 1310720 | tf_op jit(solution)/shard_map/all_gather | solution.py:42
  9.7 9.8 %collective-permute-start = (bf16[512,256]{1,0:T(8,128)(2,1)}, bf16[512,256]{1,0:T(8,128)(2,1)S(1)}, u32[]{:S(2)}, u32[]{:S(2)}) collective-permute-start(bf16[512,256]{1,0:T(8,128)(2,1)} %get-tuple-element.6), channel_id=1, source_target_pairs={{0,24},{8,0},{16,8},{24,16},{1,25},{9,1},{17,9},{25,17},{2,26},{10... | collective-permute-start | bytes 786440 | tf_op jit(solution)/shard_map/ppermute | solution.py:14
  19.6 8.0 %collective-permute-start.1 = (bf16[512,256]{1,0:T(8,128)(2,1)S(1)}, bf16[512,256]{1,0:T(8,128)(2,1)S(1)}, u32[]{:S(2)}, u32[]{:S(2)}) collective-permute-start(bf16[512,256]{1,0:T(8,128)(2,1)S(1)} %collective-permute-done), channel_id=1, source_target_pairs={{0,24},{8,0},{16,8},{24,16},{1,25},{9,1},{17,9},{25,17},{2,26},{10... | collective-permute-start | bytes 786440 | tf_op jit(solution)/shard_map/ppermute | solution.py:14
  27.5 7.3 %collective-permute-start.2 = (bf16[512,256]{1,0:T(8,128)(2,1)S(1)}, bf16[512,256]{1,0:T(8,128)(2,1)S(1)}, u32[]{:S(2)}, u32[]{:S(2)}) collective-permute-start(bf16[512,256]{1,0:T(8,128)(2,1)S(1)} %collective-permute-done.1), channel_id=1, source_target_pairs={{0,24},{8,0},{16,8},{24,16},{1,25},{9,1},{17,9},{25,17},{2,26},{10... | collective-permute-start | bytes 786440 | tf_op jit(solution)/shard_map/ppermute | solution.py:14
  44.0 29.0 %copy-start = (bf16[512,256]{1,0:T(8,128)(2,1)S(1)}, bf16[512,256]{1,0:T(8,128)(2,1)}, u32[]{:S(2)}) copy-start(bf16[512,256]{1,0:T(8,128)(2,1)} %get-tuple-element.6) | copy-start | bytes 786436
Sparse Core Ops, SparseCore 0:
  9.8 33.5 all-gather.2
  47.2 25.6 all-gather.4
